TPU v7x, 32 devices: a whole 2x2x4 slice. The times are simulated.
32 devices in a mesh: expert: 4 (over y, x), dp: 8 (over z, core).
Axes of the slice: x: 2, y: 2, z: 4, core: 2. Of those that a mesh axis runs over, the one named last changes fastest.
Arguments:
- routes: int32 [4096, 2], P(('expert', 'dp')), may hold values from 0 to 1, as said below
- expert_inputs: bfloat16 [8, 4, 512, 2048], P('dp', 'expert'), may hold values from -6 to 6
- hidden_grad: bfloat16 [8, 4, 512, 2048], P('dp', 'expert'), may hold values from -6 to 6
- weight: float32 [2048, 8192], P('dp', 'expert'), may hold values from -0.125 to 0.125
- moment_one: float32 [2048, 8192], P('dp', 'expert'), may hold values from -6 to 6
- moment_two: float32 [2048, 8192], P('dp', 'expert'), may hold values from 0.5 to 4
Outputs:
- token_grad: bfloat16 [4096, 2048], P(('expert', 'dp'))
- new_weight: float32 [2048, 8192], P('dp', 'expert')
- new_first: float32 [2048, 8192], P('dp', 'expert')
- new_second: float32 [2048, 8192], P('dp', 'expert')
Inputs may be any that keep to these rules, and one draw needn't show every extreme that they name: `routes`: each token names 2 different experts; the tokens of one device name one expert at most 128 times, and in every device's tokens some expert is named exactly 128 times.
All inputs are finite; a program needn't handle non-finite values.
Results may differ from a plain program's by a relative error of at most 0.0045.
The roundings to bfloat16 on the way count: a program that leaves them out, or rounds other values in their place, can miss the bound.
Values may be sent and summed in bfloat16 or wider, within the bound.
No kernel may reach another device: no remote copies, remote signals or barrier semaphores. Data moves between devices by JAX's collectives and lax.ppermute only.
A program may use at most 128 MiB of HBM per device.

v0:
```python
import jax
import jax.numpy as jnp
from jax import lax
from jax.sharding import PartitionSpec as P

beta_one = 0.9
beta_two = 0.95
learn_rate = 0.003
decay = 0.1
epsilon = 1e-08
loss_scale = 64.0
bias_one = 1.0 - (0.9**50) ** 2
bias_two = 1.0 - (0.95**50) ** 2


def adamw(weight, moment_one, moment_two, grad):
    new_first = beta_one * moment_one + (1.0 - beta_one) * grad
    new_second = beta_two * moment_two + (1.0 - beta_two) * grad * grad
    update = new_first / bias_one / (jnp.sqrt(new_second / bias_two) + epsilon)
    new_weight = weight - learn_rate * (update + decay * weight)
    return (new_weight, new_first, new_second)


def shards(routes, expert_inputs, hidden_grad, weight, moment_one, moment_two):
    n_expert = lax.axis_size("expert")
    experts = n_expert // 2
    slot_rows = expert_inputs.shape[2]
    capacity = slot_rows // n_expert
    width = expert_inputs.shape[3]
    tok_count = routes.shape[0]
    top_count = routes.shape[1]
    flat_routes = routes.reshape(-1)
    onehot = (flat_routes[:, None] == jnp.arange(experts, dtype=jnp.int32)[None, :]).astype(
        jnp.int32
    )
    running = jnp.cumsum(onehot, axis=0)
    slots = jnp.sum((running - 1) * onehot, axis=1).reshape(tok_count, top_count)
    counts = jnp.sum(onehot, axis=0)
    all_counts = lax.all_gather(counts[None, :], "expert", axis=0, tiled=True)
    my_expert = lax.axis_index("expert") // 2
    chosen = jnp.arange(experts, dtype=jnp.int32)[None, :] == my_expert
    my_counts = jnp.sum(jnp.where(chosen, all_counts, 0), axis=1)
    valid = (jnp.arange(capacity, dtype=jnp.int32)[None, :] < my_counts[:, None]).reshape(-1)
    inputs_flat = expert_inputs.reshape(slot_rows, width)
    grad_flat = hidden_grad.reshape(slot_rows, -1)
    masked = jnp.where(valid[:, None], grad_flat, jnp.zeros_like(grad_flat))
    wbf = weight.astype(jnp.bfloat16)
    partial_rows = lax.dot_general(
        masked,
        lax.all_gather(wbf, "dp", axis=0, tiled=True),
        (((1,), (1,)), ((), ())),
        preferred_element_type=jnp.float32,
    )
    sent = partial_rows.reshape(n_expert, capacity, width)
    received = lax.all_to_all(sent, "expert", split_axis=0, concat_axis=0, tiled=True)
    paired = jnp.sum(received.reshape(experts, 2, capacity, width), axis=1).astype(jnp.bfloat16)
    picked = paired[routes, slots]
    token_grad = jnp.sum(picked.astype(jnp.float32), axis=1).astype(jnp.bfloat16)
    owned = lax.psum_scatter(
        lax.dot_general(
            inputs_flat, masked, (((0,), (0,)), ((), ())), preferred_element_type=jnp.float32
        ).astype(jnp.bfloat16),
        "dp",
        scatter_dimension=0,
        tiled=True,
    ).astype(jnp.float32)
    new_weight, new_first, new_second = adamw(weight, moment_one, moment_two, owned / loss_scale)
    return (token_grad, new_weight, new_first, new_second)


def solution(mesh):
    in_specs = (
        P(("expert", "dp"), None),
        P("dp", "expert", None, None),
        P("dp", "expert", None, None),
        P("dp", "expert"),
        P("dp", "expert"),
        P("dp", "expert"),
    )
    out_specs = (P(("expert", "dp"), None), P("dp", "expert"), P("dp", "expert"), P("dp", "expert"))
    return jax.shard_map(shards, mesh=mesh, in_specs=in_specs, out_specs=out_specs, check_vma=False)
```

profile of v0, /device:TPU:0, one launch (start us, length us, event | category | flops | bytes accessed | tf_op | source)
XLA Modules:
  0.0 221.4 jit_solution(1023216353679421165)
XLA Ops:
  7.2 2.9 %convert_element_type.25 = bf16[256,2048]{1,0:T(8,128)(2,1)} convert(f32[256,2048]{1,0:T(8,128)} %param.9) | non-fusion elementwise | flops 524288 | bytes 3145728 | tf_op jit(solution)/shard_map/convert_element_type | solution.py:47
  10.2 0.1 copy.31
  10.3 0.1 eq.42
  10.4 0.1 eq.38
  10.6 0.6 reduce-window.6
  11.2 0.2 slice_reduce_fusion
  11.4 0.2 reduce-window.9
  11.6 0.6 dynamic-slice
  12.9 0.1 fusion.14
  13.1 0.2 dynamic-update-slice
  13.3 8.8 %all-reduce = s32[8]{0:T(128)S(1)} all-reduce(s32[8]{0:T(128)S(1)} %dynamic-update-slice), channel_id=2, replica_groups=mesh['expert'=4,'dp'=8] {'expert'}, use_global_device_ids=true, to_apply=%add | all-reduce | flops 8 | bytes 64
  22.1 0.1 reshape.114
  22.2 0.1 select_reduce_fusion
  22.4 8.8 %convert_bitcast_fusion = bf16[2048,2048]{0,1:T(8,128)(2,1)} fusion(bf16[1,1,512,2048]{3,2,1,0:T(8,128)(2,1)S(1)} %copy-done, bf16[1,1,512,2048]{3,2,1,0:T(8,128)(2,1)} %param.8, pred[512]{0:T(512)(128)(4,1)S(1)} %get-tuple-element.21), kind=kOutput, calls=%fused_computation.3 | convolution fusion | flops 4300210176 | bytes 12583424 | tf_op jit(solution)/shard_map/dot_general | solution.py:60
  31.2 63.8 %all-gather.3.cloned.1.call-done = bf16[2048,2048]{1,0:T(8,128)(2,1)} async-done(((bf16[256,2048]{1,0:T(8,128)(2,1)}), bf16[2048,2048]{1,0:T(8,128)(2,1)}) %all-gather.3.cloned.1.call-update) | async-done | bytes 8388624 | tf_op jit(solution)/shard_map/all_gather | solution.py:50
  95.0 10.5 %fusion = f32[4,128,2048]{2,1,0:T(8,128)} fusion(bf16[2048,2048]{1,0:T(8,128)(2,1)} %all-gather.3.cloned.1.call-done, bf16[4,128,2048]{2,1,0:T(8,128)(2,1)} %bitcast.39, pred[4,128]{1,0:T(4,128)(4,1)S(1)} %get-tuple-element.22), kind=kOutput, calls=%fused_computation.1 | convolution fusion | flops 4296015872 | bytes 14680576 | tf_op jit(solution)/shard_map/dot_general | solution.py:48
  105.6 5.1 %all-to-all-start = ((f32[4,128,2048]{2,1,0:T(8,128)}), f32[4,128,2048]{2,1,0:T(8,128)}, u32[]{:S(2)}, u32[]{:S(2)}) async-start(f32[4,128,2048]{2,1,0:T(8,128)} %fusion), calls=%async_computation | async-start | bytes 8388608 | tf_op jit(solution)/shard_map/all_to_all | solution.py:55
  110.7 2.9 %copy.40 = f32[256,2048]{0,1:T(8,128)} copy(f32[256,2048]{1,0:T(8,128)} %param.9) | data formatting | bytes 4194304 | tf_op args[3]
  113.6 0.1 reshape.106
  113.8 0.1 copy.36
  113.9 0.1 reshape.108
  114.1 2.9 %copy.37 = f32[256,2048]{0,1:T(8,128)} copy(f32[256,2048]{1,0:T(8,128)} %param.10) | data formatting | bytes 4194304 | tf_op args[4]
  117.0 2.9 %copy.38 = f32[256,2048]{0,1:T(8,128)} copy(f32[256,2048]{1,0:T(8,128)} %param.11) | data formatting | bytes 4194304 | tf_op args[5]
  119.9 65.6 %reduce-scatter.2.cloned.1.call-done = bf16[256,2048]{0,1:T(8,128)(2,1)} async-done(((bf16[2048,2048]{0,1:T(8,128)(2,1)}), bf16[256,2048]{0,1:T(8,128)(2,1)}) %reduce-scatter.2.cloned.1.call-update) | async-done | bytes 1048592 | tf_op jit(solution)/shard_map/reduce_scatter | solution.py:59
  185.5 7.0 %multiply_subtract_fusion = (f32[256,2048]{0,1:T(8,128)}, f32[256,2048]{0,1:T(8,128)}, f32[256,2048]{0,1:T(8,128)}) fusion(f32[256,2048]{0,1:T(8,128)} %copy.40, bf16[256,2048]{0,1:T(8,128)(2,1)} %reduce-scatter.2.cloned.1.call-done, f32[256,2048]{0,1:T(8,128)} %copy.37, f32[256,2048]{0,1:T(8,128)} %copy.38), kind=kLoop, calls=%fused_computation.13 | loop fusion | flops 8912896 | bytes 13631488 | tf_op jit(solution)/shard_map/sub | solution.py:20
  192.5 2.9 %copy.41 = f32[256,2048]{1,0:T(8,128)} copy(f32[256,2048]{0,1:T(8,128)} %get-tuple-element.18) | data formatting | bytes 4194304
  195.4 2.9 %copy.42 = f32[256,2048]{1,0:T(8,128)} copy(f32[256,2048]{0,1:T(8,128)} %get-tuple-element.19) | data formatting | bytes 4194304
  198.2 2.9 %copy.43 = f32[256,2048]{1,0:T(8,128)} copy(f32[256,2048]{0,1:T(8,128)} %get-tuple-element.20) | data formatting | bytes 4194304
  201.1 2.7 %bitcast_reduce_fusion = bf16[2,128,2048]{2,1,0:T(8,128)(2,1)S(1)} fusion(f32[4,128,2048]{2,1,0:T(8,128)} %all-to-all-done), kind=kLoop, calls=%fused_computation.4 | loop fusion | flops 524288 | bytes 5242880 | tf_op jit(solution)/shard_map/reduce_sum | solution.py:56
  203.9 5.3 %gather_fusion = bf16[256,2048]{1,0:T(8,128)(2,1)} fusion(bf16[2,128,2048]{2,1,0:T(8,128)(2,1)S(1)} %bitcast_reduce_fusion, s32[256]{0:T(256)S(1)} %reshape.108), kind=kCustom, calls=%fused_computation | custom fusion | bytes 2099200 | tf_op jit(solution)/shard_map/gather | solution.py:57
  209.2 1.7 reshape.111
  210.9 3.6 %reduce_sum.52 = bf16[128,2048]{1,0:T(8,128)(2,1)} reduce(bf16[128,2,2048]{2,1,0:T(2,128)(2,1)S(1)} %reshape.111, bf16[]{:T(256)} %constant.46.clone.1), dimensions={1}, to_apply=%region_6.7 | reduce | flops 262144 | bytes 1572866 | tf_op jit(solution)/shard_map/reduce_sum | solution.py:58
  (18 shorter events, 0.4 us)
Async XLA Ops:
  7.2 15.2 %copy-start = (bf16[1,1,512,2048]{3,2,1,0:T(8,128)(2,1)S(1)}, bf16[1,1,512,2048]{3,2,1,0:T(8,128)(2,1)}, u32[]{:S(2)}) copy-start(bf16[1,1,512,2048]{3,2,1,0:T(8,128)(2,1)} %param.7) | copy-start | bytes 6291460
  7.2 4.4 %copy-start.2 = (u32[32]{0:T(128)S(1)}, u32[32]{0:T(128)}, u32[]{:S(2)}) copy-start(u32[32]{0:T(128)} %constant.77) | copy-start | bytes 388
  7.2 3.0 %copy-start.1 = (s32[128,2]{0,1:T(2,128)S(1)}, s32[128,2]{0,1:T(2,128)}, u32[]{:S(2)}) copy-start(s32[128,2]{0,1:T(2,128)} %param.6) | copy-start | bytes 3076
  7.2 87.8 %all-gather.3.cloned.1.call-start = ((), (), s32[]{:S(2)}) async-start(), calls=%async_computation.2 | async-start | bytes 9437184 | tf_op jit(solution)/shard_map/all_gather | solution.py:50
  10.1 175.4 %reduce-scatter.2.cloned.1.call-start = ((), (), s32[]{:S(2)}) async-start(), calls=%async_computation.3 | async-start | bytes 9437184 | tf_op jit(solution)/shard_map/reduce_scatter | solution.py:59
  105.6 95.5 %all-to-all-start = ((f32[4,128,2048]{2,1,0:T(8,128)}), f32[4,128,2048]{2,1,0:T(8,128)}, u32[]{:S(2)}, u32[]{:S(2)}) async-start(f32[4,128,2048]{2,1,0:T(8,128)} %fusion), calls=%async_computation | async-start | bytes 8388608 | tf_op jit(solution)/shard_map/all_to_all | solution.py:55
Sparse Core Ops, SparseCore 0:
  10.2 84.7 all-gather.2
  97.3 88.1 reduce-scatter.1
where the time goes:
time: 222 us; the launch traced here: 221 us
  waiting for transfers between devices  129 us (58%)
  local copies, waits for them, and re-layouts  26.4 us (12%)
  matrix products  19.4 us (9%)
  other arithmetic  17.4 us (8%)
  between operations  14.8 us (7%)
  blocking collectives  8.82 us (4%)
  starting transfers between devices  5.2 us (2%)
    reduce_scatter x1, waiting for transfers between devices, shards(): lax.psum_scatter(lax.dot_general(inputs_flat, masked, (((0,), (0,)), ((),...  65.6 us
    all_gather x1, waiting for transfers between devices, shards(): lax.all_gather(wbf, 'dp', axis=0, tiled=True)  63.8 us
    unnamed x16, local copies, waits for them, and re-layouts  18.3 us
    dot_general x1, matrix products, shards(): lax.dot_general(masked, lax.all_gather(wbf, 'dp', axis=0, tiled=True), ((...  10.5 us
    unnamed x1, blocking collectives  8.82 us
    dot_general x1, matrix products, shards(): lax.dot_general(inputs_flat, masked, (((0,), (0,)), ((), ())), preferred_...  8.81 us
    gather x2, local copies, waits for them, and re-layouts, shards(): picked = paired[routes, slots]  7.06 us
    sub x1, other arithmetic, adamw(): new_weight = weight - learn_rate * (update + decay * weight)  6.97 us
  transfers between devices with their start and end apart: 3, of which 2 were waited for; matrix products, arithmetic and copies ran while one was open for 21% of the time, Pallas kernels for 0%

commit v1 on v0

--- a/solution.py
+++ b/solution.py
@@ -11,6 +11,28 @@
 loss_scale = 64.0
 bias_one = 1.0 - (0.9**50) ** 2
 bias_two = 1.0 - (0.95**50) ** 2
+
+
+def in_order(blocks, dim):
+    dims = list(blocks.shape[1:])
+    dims[dim] *= blocks.shape[0]
+    return jnp.moveaxis(blocks, 0, dim).reshape(dims)
+
+
+def gather_around(array, axis, dim):
+    count = lax.axis_size(axis)
+    pairs = [(i, (i + 1) % count) for i in range(count)]
+    back = [(b, a) for a, b in pairs]
+    lower, upper = ([], [])
+    for step in range(count - 1):
+        if step % 2 == 0:
+            lower.append(lax.ppermute(lower[-1] if lower else array, axis, pairs))
+        else:
+            upper.append(lax.ppermute(upper[-1] if upper else array, axis, back))
+    blocks = jnp.stack([*lower[::-1], array, *upper])
+    shift = lax.axis_index(axis) - len(lower)
+    blocks = blocks[(jnp.arange(count) - shift) % count]
+    return in_order(blocks, dim)
 
 
 def adamw(weight, moment_one, moment_two, grad):
@@ -47,7 +69,7 @@
     wbf = weight.astype(jnp.bfloat16)
     partial_rows = lax.dot_general(
         masked,
-        lax.all_gather(wbf, "dp", axis=0, tiled=True),
+        gather_around(wbf, "dp", 0),
         (((1,), (1,)), ((), ())),
         preferred_element_type=jnp.float32,
     )

time: 222 us -> 310 us (1.40)
  waiting for transfers between devices: 129 us -> 186 us
  local copies, waits for them, and re-layouts: 26.4 us -> 48.9 us
  starting transfers between devices: 5.2 us -> 15.6 us
    ppermute x0 -> x7, waiting for transfers between devices: none -> 151 us  [the longest x4 150 us: gather_around(): lower.append(lax.ppermute(lower[-1] if lower else array, axis, pairs))]
    reduce_scatter x1, waiting for transfers between devices: 65.6 us -> 0.01 us  [shards(): lax.psum_scatter(lax.dot_general(inputs_flat, masked, (((0,), (0,)), ((),...]
    all_gather x1 -> x0, waiting for transfers between devices: 63.8 us -> none  [shards(): lax.all_gather(wbf, 'dp', axis=0, tiled=True)]
    all_to_all x1, waiting for transfers between devices: 0.01 us -> 35.3 us  [shards(): lax.all_to_all(sent, 'expert', split_axis=0, concat_axis=0, tiled=True)]
    unnamed x16 -> x34, local copies, waits for them, and re-layouts: 18.3 us -> 32.8 us
    ppermute x0 -> x7, starting transfers between devices: none -> 10.5 us  [the longest x3 10.4 us: gather_around(): upper.append(lax.ppermute(upper[-1] if upper else array, axis, back))]
    gather x0 -> x1, local copies, waits for them, and re-layouts: none -> 8.05 us  [gather_around(): blocks = blocks[(jnp.arange(count) - shift) % count]]
  transfers between devices with their start and end apart: 3 -> 9, of which waited for: 2 -> 7; matrix products, arithmetic and copies ran while one was open for 21% -> 17% of each run, Pallas kernels for 0% -> 0%
where the time goes in v1:
time: 310 us
  waiting for transfers between devices  186 us (60%)
  local copies, waits for them, and re-layouts  48.9 us (16%)
  other arithmetic  18 us (6%)
  matrix products  17.4 us (6%)
  starting transfers between devices  15.6 us (5%)
  between operations  14.9 us (5%)
  blocking collectives  8.83 us (3%)
    ppermute x4, waiting for transfers between devices, gather_around(): lower.append(lax.ppermute(lower[-1] if lower else array, axis, pairs))  150 us
    all_to_all x1, waiting for transfers between devices, shards(): lax.all_to_all(sent, 'expert', split_axis=0, concat_axis=0, tiled=True)  35.3 us
    unnamed x34, local copies, waits for them, and re-layouts  32.8 us
    dot_general x1, matrix products, shards(): lax.dot_general(masked, gather_around(wbf, 'dp', 0), (((1,), (1,)), ((),...  10.5 us
    ppermute x3, starting transfers between devices, gather_around(): upper.append(lax.ppermute(upper[-1] if upper else array, axis, back))  10.4 us
    unnamed x1, blocking collectives  8.83 us
    gather x1, local copies, waits for them, and re-layouts, gather_around(): blocks = blocks[(jnp.arange(count) - shift) % count]  8.05 us
    dot_general x1, matrix products, shards(): lax.dot_general(inputs_flat, masked, (((0,), (0,)), ((), ())), preferred_...  6.83 us
  transfers between devices with their start and end apart: 9, of which 7 were waited for; matrix products, arithmetic and copies ran while one was open for 17% of the time, Pallas kernels for 0%

profile of v1, /device:TPU:0, one launch (start us, length us, event | category | flops | bytes accessed | tf_op | source)
XLA Modules:
  0.0 309.8 jit_solution(15714090881878481912)
XLA Ops:
  9.7 1.2 dynamic-slice
  11.8 8.8 %all-reduce = s32[8]{0:T(128)S(1)} all-reduce(s32[8]{0:T(128)S(1)} %dynamic-update-slice), channel_id=2, replica_groups=mesh['expert'=4,'dp'=8] {'expert'}, use_global_device_ids=true, to_apply=%add | all-reduce | flops 8 | bytes 64
  20.9 1.8 broadcast_select_fusion
  22.8 1.3 copy-done.5
  24.1 6.8 %convert_bitcast_fusion = bf16[2048,2048]{0,1:T(8,128)(2,1)} fusion(bf16[1,1,512,2048]{3,2,1,0:T(8,128)(2,1)S(1)} %copy-done, bf16[1,1,512,2048]{3,2,1,0:T(8,128)(2,1)S(1)} %broadcast_select_fusion), kind=kOutput, calls=%fused_computation.2 | convolution fusion | flops 4299161600 | bytes 12582912 | tf_op jit(solution)/shard_map/dot_general | solution.py:82
  30.9 1.6 copy-done.2
  32.7 30.9 %collective-permute-done = bf16[256,2048]{1,0:T(8,128)(2,1)S(1)} collective-permute-done((bf16[256,2048]{1,0:T(8,128)(2,1)S(1)}, bf16[256,2048]{1,0:T(8,128)(2,1)S(1)}, u32[]{:S(2)}, u32[]{:S(2)}) %collective-permute-start) | collective-permute-done | bytes 1048608 | tf_op jit(solution)/shard_map/ppermute | solution.py:29
  63.7 3.5 %collective-permute-start.4 = (bf16[256,2048]{1,0:T(8,128)(2,1)S(1)}, bf16[256,2048]{1,0:T(8,128)(2,1)}, u32[]{:S(2)}, u32[]{:S(2)}) collective-permute-start(bf16[256,2048]{1,0:T(8,128)(2,1)S(1)} %convert_element_type.25), channel_id=1, source_target_pairs={{1,0},{2,1},{3,2},{4,3},{5,4},{6,5},{7,6},{0,7},{9,8},{10,9},{11,1... | collective-permute-start | bytes 3145736 | tf_op jit(solution)/shard_map/ppermute | solution.py:31
  67.2 45.3 %collective-permute-done.1 = bf16[256,2048]{1,0:T(8,128)(2,1)S(1)} collective-permute-done((bf16[256,2048]{1,0:T(8,128)(2,1)S(1)}, bf16[256,2048]{1,0:T(8,128)(2,1)S(1)}, u32[]{:S(2)}, u32[]{:S(2)}) %collective-permute-start.1) | collective-permute-done | bytes 1048608 | tf_op jit(solution)/shard_map/ppermute | solution.py:29
  113.5 3.2 %collective-permute-start.5 = (bf16[256,2048]{1,0:T(8,128)(2,1)}, bf16[256,2048]{1,0:T(8,128)(2,1)}, u32[]{:S(2)}, u32[]{:S(2)}) collective-permute-start(bf16[256,2048]{1,0:T(8,128)(2,1)} %collective-permute-done.4), channel_id=1, source_target_pairs={{1,0},{2,1},{3,2},{4,3},{5,4},{6,5},{7,6},{0,7},{9,8},{10,9},{11,1... | collective-permute-start | bytes 3145736 | tf_op jit(solution)/shard_map/ppermute | solution.py:31
  116.6 45.1 %collective-permute-done.2 = bf16[256,2048]{1,0:T(8,128)(2,1)} collective-permute-done((bf16[256,2048]{1,0:T(8,128)(2,1)S(1)}, bf16[256,2048]{1,0:T(8,128)(2,1)}, u32[]{:S(2)}, u32[]{:S(2)}) %collective-permute-start.2) | collective-permute-done | bytes 1048608 | tf_op jit(solution)/shard_map/ppermute | solution.py:29
  162.0 3.7 %collective-permute-start.6 = (bf16[256,2048]{1,0:T(8,128)(2,1)}, bf16[256,2048]{1,0:T(8,128)(2,1)S(1)}, u32[]{:S(2)}, u32[]{:S(2)}) collective-permute-start(bf16[256,2048]{1,0:T(8,128)(2,1)} %collective-permute-done.5), channel_id=1, source_target_pairs={{1,0},{2,1},{3,2},{4,3},{5,4},{6,5},{7,6},{0,7},{9,8},{10,9},{11,1... | collective-permute-start | bytes 3145736 | tf_op jit(solution)/shard_map/ppermute | solution.py:31
  165.7 29.0 %collective-permute-done.3 = bf16[256,2048]{1,0:T(8,128)(2,1)} collective-permute-done((bf16[256,2048]{1,0:T(8,128)(2,1)}, bf16[256,2048]{1,0:T(8,128)(2,1)}, u32[]{:S(2)}, u32[]{:S(2)}) %collective-permute-start.3) | collective-permute-done | bytes 1048608 | tf_op jit(solution)/shard_map/ppermute | solution.py:29
  194.7 2.4 bitcast_dynamic-update-slice_fusion.7
  197.1 2.3 bitcast_dynamic-update-slice_fusion.6
  202.7 2.3 bitcast_dynamic-update-slice_fusion.2
  205.0 2.3 bitcast_dynamic-update-slice_fusion.1
  208.4 8.1 %gather_fusion = bf16[8,256,2048]{2,1,0:T(8,128)(2,1)} fusion(bf16[8,256,2048]{2,1,0:T(8,128)(2,1)} %bitcast_dynamic-update-slice_fusion, s32[1024]{0:T(1024)S(1)} %pad_clamp_fusion), kind=kCustom, calls=%fused_computation | custom fusion | bytes 16777248 | tf_op jit(solution)/shard_map/gather | solution.py:34
  216.4 10.5 %fusion.18 = f32[4,128,2048]{2,1,0:T(8,128)} fusion(bf16[4,128,2048]{2,1,0:T(8,128)(2,1)} %bitcast.59, bf16[2048,2048,1]{1,0,2:T(8,128)(2,1)} %bitcast.58), kind=kOutput, calls=%fused_computation.49 | convolution fusion | flops 4294967296 | bytes 14680064 | tf_op jit(solution)/shard_map/dot_general | solution.py:70
  227.0 5.1 %all-to-all-start = ((f32[4,128,2048]{2,1,0:T(8,128)}), f32[4,128,2048]{2,1,0:T(8,128)}, u32[]{:S(2)}, u32[]{:S(2)}) async-start(f32[4,128,2048]{2,1,0:T(8,128)} %fusion.18), calls=%async_computation | async-start | bytes 8388608 | tf_op jit(solution)/shard_map/all_to_all | solution.py:77
  232.1 1.8 copy.40
  234.4 2.9 copy.37
  237.3 2.9 copy.38
  240.2 35.3 %all-to-all-done = f32[4,128,2048]{2,1,0:T(8,128)} async-done(((f32[4,128,2048]{2,1,0:T(8,128)}), f32[4,128,2048]{2,1,0:T(8,128)}, u32[]{:S(2)}, u32[]{:S(2)}) %all-to-all-start) | async-done | bytes 4194336 | tf_op jit(solution)/shard_map/all_to_all | solution.py:77
  275.5 2.7 bitcast_reduce_fusion
  278.2 4.3 %gather_fusion.1 = bf16[256,2048]{1,0:T(8,128)(2,1)S(1)} fusion(bf16[2,128,2048]{2,1,0:T(8,128)(2,1)S(1)} %bitcast_reduce_fusion, s32[256]{0:T(256)S(1)} %reshape.177), kind=kCustom, calls=%fused_computation.1 | custom fusion | bytes 2099200 | tf_op jit(solution)/shard_map/gather | solution.py:79
  282.6 1.6 reshape.180
  284.1 4.6 %reduce_sum.52 = bf16[128,2048]{1,0:T(8,128)(2,1)} reduce(bf16[128,2,2048]{2,1,0:T(2,128)(2,1)} %reshape.180, bf16[]{:T(256)} %constant.64.clone.1), dimensions={1}, to_apply=%region_6.7 | reduce | flops 262144 | bytes 1572866 | tf_op jit(solution)/shard_map/reduce_sum | solution.py:80
  288.7 6.3 %multiply_subtract_fusion = (f32[256,2048]{0,1:T(8,128)}, f32[256,2048]{0,1:T(8,128)}, f32[256,2048]{0,1:T(8,128)}) fusion(f32[256,2048]{0,1:T(8,128)S(1)} %copy-done.3, bf16[256,2048]{0,1:T(8,128)(2,1)} %reduce-scatter.2.cloned.1.call-done, f32[256,2048]{0,1:T(8,128)} %copy.37, f32[256,2048]{0,1:T(8,128)} %copy.38), kind=kLoop, calls=%fused_computation.12 | loop fusion | flops 8912896 | bytes 13631488 | tf_op jit(solution)/shard_map/sub | solution.py:42
  295.0 3.0 copy.41
  298.1 1.8 copy.42
  299.9 3.0 copy.43
  (53 shorter events, 9.3 us)
Async XLA Ops:
  7.2 16.9 %copy-start = (bf16[1,1,512,2048]{3,2,1,0:T(8,128)(2,1)S(1)}, bf16[1,1,512,2048]{3,2,1,0:T(8,128)(2,1)}, u32[]{:S(2)}) copy-start(bf16[1,1,512,2048]{3,2,1,0:T(8,128)(2,1)} %param.7) | copy-start | bytes 6291460
  7.2 281.5 %reduce-scatter.2.cloned.1.call-start = ((), (), s32[]{:S(2)}) async-start(), calls=%async_computation.2 | async-start | bytes 9437184 | tf_op jit(solution)/shard_map/reduce_scatter | solution.py:81
  22.8 1.3 copy-start.5
  30.9 1.6 copy-start.2
  32.7 31.0 %collective-permute-start = (bf16[256,2048]{1,0:T(8,128)(2,1)S(1)}, bf16[256,2048]{1,0:T(8,128)(2,1)S(1)}, u32[]{:S(2)}, u32[]{:S(2)}) collective-permute-start(bf16[256,2048]{1,0:T(8,128)(2,1)S(1)} %convert_element_type.25), channel_id=1, source_target_pairs={{0,1},{1,2},{2,3},{3,4},{4,5},{5,6},{6,7},{7,0},{8,9},{9,10},{10,1... | collective-permute-start | bytes 3145736 | tf_op jit(solution)/shard_map/ppermute | solution.py:29
  63.6 48.9 %collective-permute-start.1 = (bf16[256,2048]{1,0:T(8,128)(2,1)S(1)}, bf16[256,2048]{1,0:T(8,128)(2,1)S(1)}, u32[]{:S(2)}, u32[]{:S(2)}) collective-permute-start(bf16[256,2048]{1,0:T(8,128)(2,1)S(1)} %collective-permute-done), channel_id=1, source_target_pairs={{0,1},{1,2},{2,3},{3,4},{4,5},{5,6},{6,7},{7,0},{8,9},{9,10},{10,1... | collective-permute-start | bytes 3145736 | tf_op jit(solution)/shard_map/ppermute | solution.py:29
  63.7 49.1 %collective-permute-start.4 = (bf16[256,2048]{1,0:T(8,128)(2,1)S(1)}, bf16[256,2048]{1,0:T(8,128)(2,1)}, u32[]{:S(2)}, u32[]{:S(2)}) collective-permute-start(bf16[256,2048]{1,0:T(8,128)(2,1)S(1)} %convert_element_type.25), channel_id=1, source_target_pairs={{1,0},{2,1},{3,2},{4,3},{5,4},{6,5},{7,6},{0,7},{9,8},{10,9},{11,1... | collective-permute-start | bytes 3145736 | tf_op jit(solution)/shard_map/ppermute | solution.py:31
  112.5 1.0 copy-start.6
  112.5 49.2 %collective-permute-start.2 = (bf16[256,2048]{1,0:T(8,128)(2,1)S(1)}, bf16[256,2048]{1,0:T(8,128)(2,1)}, u32[]{:S(2)}, u32[]{:S(2)}) collective-permute-start(bf16[256,2048]{1,0:T(8,128)(2,1)S(1)} %collective-permute-done.1), channel_id=1, source_target_pairs={{0,1},{1,2},{2,3},{3,4},{4,5},{5,6},{6,7},{7,0},{8,9},{9,10},{10,1... | collective-permute-start | bytes 3145736 | tf_op jit(solution)/shard_map/ppermute | solution.py:29
  113.5 48.5 %collective-permute-start.5 = (bf16[256,2048]{1,0:T(8,128)(2,1)}, bf16[256,2048]{1,0:T(8,128)(2,1)}, u32[]{:S(2)}, u32[]{:S(2)}) collective-permute-start(bf16[256,2048]{1,0:T(8,128)(2,1)} %collective-permute-done.4), channel_id=1, source_target_pairs={{1,0},{2,1},{3,2},{4,3},{5,4},{6,5},{7,6},{0,7},{9,8},{10,9},{11,1... | collective-permute-start | bytes 3145736 | tf_op jit(solution)/shard_map/ppermute | solution.py:31
  161.7 33.0 %collective-permute-start.3 = (bf16[256,2048]{1,0:T(8,128)(2,1)}, bf16[256,2048]{1,0:T(8,128)(2,1)}, u32[]{:S(2)}, u32[]{:S(2)}) collective-permute-start(bf16[256,2048]{1,0:T(8,128)(2,1)} %collective-permute-done.2), channel_id=1, source_target_pairs={{0,1},{1,2},{2,3},{3,4},{4,5},{5,6},{6,7},{7,0},{8,9},{9,10},{10,1... | collective-permute-start | bytes 3145736 | tf_op jit(solution)/shard_map/ppermute | solution.py:29
  161.8 37.7 %copy-start.7 = (bf16[256,2048]{1,0:T(8,128)(2,1)S(1)}, bf16[256,2048]{1,0:T(8,128)(2,1)}, u32[]{:S(2)}) copy-start(bf16[256,2048]{1,0:T(8,128)(2,1)} %copy-done.6) | copy-start | bytes 3145732
  162.0 45.4 %collective-permute-start.6 = (bf16[256,2048]{1,0:T(8,128)(2,1)}, bf16[256,2048]{1,0:T(8,128)(2,1)S(1)}, u32[]{:S(2)}, u32[]{:S(2)}) collective-permute-start(bf16[256,2048]{1,0:T(8,128)(2,1)} %collective-permute-done.5), channel_id=1, source_target_pairs={{1,0},{2,1},{3,2},{4,3},{5,4},{6,5},{7,6},{0,7},{9,8},{10,9},{11,1... | collective-permute-start | bytes 3145736 | tf_op jit(solution)/shard_map/ppermute | solution.py:31
  227.0 48.5 %all-to-all-start = ((f32[4,128,2048]{2,1,0:T(8,128)}), f32[4,128,2048]{2,1,0:T(8,128)}, u32[]{:S(2)}, u32[]{:S(2)}) async-start(f32[4,128,2048]{2,1,0:T(8,128)} %fusion.18), calls=%async_computation | async-start | bytes 8388608 | tf_op jit(solution)/shard_map/all_to_all | solution.py:77
  232.1 2.0 copy-start.8
  282.5 6.2 %copy-start.3 = (f32[256,2048]{0,1:T(8,128)S(1)}, f32[256,2048]{0,1:T(8,128)}, u32[]{:S(2)}) copy-start(f32[256,2048]{0,1:T(8,128)} %copy.40) | copy-start | bytes 6291460
  295.0 3.0 copy-start.4
  299.9 3.0 copy-start.1
Sparse Core Ops, SparseCore 0:
  31.1 147.8 reduce-scatter.1
